TPU v7x, 32 devices: a whole 2x2x4 slice. The times are simulated.
32 devices in a mesh: rows: 4 (over y, x), cols: 8 (over z, core).
Axes of the slice: x: 2, y: 2, z: 4, core: 2. Of those that a mesh axis runs over, the one named last changes fastest.
Arguments:
- features: bfloat16 [32, 128, 1024], P('rows', 'cols'), may hold values from -24 to 24
- w_query: bfloat16 [1024, 1024], replicated, may hold values from -0.1875 to 0.1875
- w_key: bfloat16 [1024, 1024], replicated, may hold values from -0.1875 to 0.1875
- w_value: bfloat16 [1024, 1024], replicated, may hold values from -0.1875 to 0.1875
- w_out: bfloat16 [1024, 1024], replicated, may hold values from -0.1875 to 0.1875
- reg_pos: int32 [32], replicated, may hold values from 0 to 4095, as said below
- grad_out: bfloat16 [32, 128, 1024], P('rows', 'cols'), may hold values from -6 to 6
Outputs:
- layer_out: bfloat16 [32, 128, 1024], P('rows', 'cols')
- grad_in: bfloat16 [32, 128, 1024], P('rows', 'cols')
Inputs may be any that keep to these rules, and one draw needn't show every extreme that they name: The 32 global tokens are distinct, one in each tile of 128 tokens: reg_pos[r] lies in tile row r // 8 and tile column r % 8, tiles counted row by row.
All inputs are finite; a program needn't handle non-finite values.
Results may differ from a plain program's by a relative error of at most 0.03.
The roundings to bfloat16 on the way count: a program that leaves them out, or rounds other values in their place, can miss the bound.
Values may be sent and summed in bfloat16 or wider, within the bound.
No kernel may reach another device: no remote copies, remote signals or barrier semaphores. Data moves between devices by JAX's collectives and lax.ppermute only.
A program may use at most 128 MiB of HBM per device.

v0:
```python
import math
import jax
import jax.numpy as jnp
from jax import lax
from jax.sharding import PartitionSpec as P

HEADS = 16
KW = 13
RAD = 6
BLK = 8


def with_halo(block, sides, width):
    for axis, dim in sides:
        count = lax.axis_size(axis)
        forward = [(i, i + 1) for i in range(count - 1)]
        backward = [(target, source) for source, target in forward]
        low = lax.ppermute(
            lax.slice_in_dim(block, block.shape[dim] - width, None, axis=dim), axis, forward
        )
        high = lax.ppermute(lax.slice_in_dim(block, 0, width, axis=dim), axis, backward)
        block = jnp.concatenate([low, block, high], axis=dim)
    return block


def from_behind(x, axis, by):
    size = lax.axis_size(axis)
    pairs = [(i, i + by) for i in range(size) if 0 <= i + by < size]
    return lax.ppermute(x, axis, pairs)


def axis_mask(first_cell, extent, block_count):
    block_ids = jnp.arange(block_count, dtype=jnp.int32)[:, None, None]
    within = jnp.arange(BLK, dtype=jnp.int32)[None, :, None]
    offsets = jnp.arange(BLK + 2 * RAD, dtype=jnp.int32)[None, None, :]
    query_cell = first_cell + BLK * block_ids + within
    window_start = jnp.clip(query_cell - RAD, 0, extent - KW)
    key_cell = first_cell + BLK * block_ids - RAD + offsets
    return (key_cell >= window_start) & (key_cell <= window_start + KW - 1)


def block_mask(row_mask, col_mask):
    row_blocks = row_mask.shape[0]
    col_blocks = col_mask.shape[0]
    span_cells = BLK + 2 * RAD
    joined = row_mask[:, None, :, None, :, None] & col_mask[None, :, None, :, None, :]
    return joined.reshape(row_blocks * col_blocks, BLK * BLK, span_cells * span_cells)


def to_blocks(cell_grid, row_blocks, col_blocks):
    channels = cell_grid.shape[-1]
    shaped = cell_grid.reshape(row_blocks, BLK, col_blocks, BLK, channels).transpose(0, 2, 1, 3, 4)
    return shaped.reshape(row_blocks * col_blocks, BLK * BLK, channels)


def from_blocks(blocks, row_blocks, col_blocks):
    channels = blocks.shape[-1]
    shaped = blocks.reshape(row_blocks, col_blocks, BLK, BLK, channels).transpose(0, 2, 1, 3, 4)
    return shaped.reshape(row_blocks * BLK, col_blocks * BLK, channels)


def windows(framed, row_blocks, col_blocks):
    channels = framed.shape[-1]
    span_cells = BLK + 2 * RAD
    block_ids = jnp.arange(row_blocks * col_blocks, dtype=jnp.int32)

    def cut_box(block_id):
        top_cell = block_id // col_blocks * BLK
        left_cell = block_id % col_blocks * BLK
        box = lax.dynamic_slice(
            framed, (top_cell, left_cell, jnp.int32(0)), (span_cells, span_cells, channels)
        )
        return box.reshape(span_cells * span_cells, channels)

    return jax.vmap(cut_box)(block_ids)


def windows_adjoint(block_grads, row_blocks, col_blocks):
    channels = block_grads.shape[-1]
    span_cells = BLK + 2 * RAD
    total = jnp.zeros(
        (row_blocks * BLK + 2 * RAD, col_blocks * BLK + 2 * RAD, channels), jnp.float32
    )

    def add_box(block_id, accum):
        top_cell = block_id // col_blocks * BLK
        left_cell = block_id % col_blocks * BLK
        start = (top_cell, left_cell, jnp.int32(0))
        piece = lax.dynamic_index_in_dim(block_grads, block_id, 0, keepdims=False).reshape(
            span_cells, span_cells, channels
        )
        current = lax.dynamic_slice(accum, start, (span_cells, span_cells, channels))
        return lax.dynamic_update_slice(accum, current + piece, start)

    return lax.fori_loop(0, row_blocks * col_blocks, add_box, total)


def split_heads(query_blocks, window_kv, global_kv):
    block_count, query_count, model_width = query_blocks.shape
    head_size = model_width // HEADS
    query_heads = query_blocks.reshape(block_count, query_count, HEADS, head_size)
    window_keys = window_kv[:, :, :model_width].reshape(block_count, -1, HEADS, head_size)
    window_values = window_kv[:, :, model_width:].reshape(block_count, -1, HEADS, head_size)
    global_keys = global_kv[:, :model_width].reshape(-1, HEADS, head_size)
    global_values = global_kv[:, model_width:].reshape(-1, HEADS, head_size)
    return (query_heads, window_keys, window_values, global_keys, global_values)


def einsum_wide(form, left, right):
    return jnp.einsum(form, left, right, preferred_element_type=jnp.float32)


def forward_block(query_blocks, window_kv, global_kv, window_mask):
    block_count, query_count, model_width = query_blocks.shape
    score_scale = 1.0 / math.sqrt(model_width // HEADS)
    query_heads, window_keys, window_values, global_keys, global_values = split_heads(
        query_blocks, window_kv, global_kv
    )
    window_scores = einsum_wide("bqhd,bkhd->bhqk", query_heads, window_keys) * score_scale
    window_scores = jnp.where(window_mask[:, None], window_scores, -1e30)
    global_scores = einsum_wide("bqhd,rhd->bhqr", query_heads, global_keys) * score_scale
    row_max = jnp.maximum(
        jnp.max(window_scores, axis=-1, keepdims=True),
        jnp.max(global_scores, axis=-1, keepdims=True),
    )
    window_exp = jnp.exp(window_scores - row_max)
    global_exp = jnp.exp(global_scores - row_max)
    denominator = jnp.sum(window_exp, axis=-1, keepdims=True) + jnp.sum(
        global_exp, axis=-1, keepdims=True
    )
    window_probs = window_exp / denominator
    global_probs = global_exp / denominator
    window_rounded = window_probs.astype(jnp.bfloat16)
    global_rounded = global_probs.astype(jnp.bfloat16)
    attended = einsum_wide("bhqk,bkhd->bqhd", window_rounded, window_values) + einsum_wide(
        "bhqr,rhd->bqhd", global_rounded, global_values
    )
    attended = attended.astype(jnp.bfloat16).reshape(block_count, query_count, model_width)
    return ((window_probs, global_probs, window_rounded, global_rounded), attended)


def backward_block(query_blocks, window_kv, global_kv, probs, attended, grad_blocks):
    block_count, query_count, model_width = query_blocks.shape
    head_size = model_width // HEADS
    score_scale = 1.0 / math.sqrt(head_size)
    window_probs, global_probs, window_rounded, global_rounded = probs
    query_heads, window_keys, window_values, global_keys, global_values = split_heads(
        query_blocks, window_kv, global_kv
    )
    grad_heads = grad_blocks.reshape(block_count, query_count, HEADS, head_size)
    attended_heads = attended.reshape(block_count, query_count, HEADS, head_size)
    delta_terms = einsum_wide("bqhd,bqhd->bhq", grad_heads, attended_heads)[..., None]
    window_dots = einsum_wide("bqhd,bkhd->bhqk", grad_heads, window_values)
    global_dots = einsum_wide("bqhd,rhd->bhqr", grad_heads, global_values)
    window_slopes = (window_probs * (window_dots - delta_terms) * score_scale).astype(jnp.bfloat16)
    global_slopes = (global_probs * (global_dots - delta_terms) * score_scale).astype(jnp.bfloat16)
    query_grads = einsum_wide("bhqk,bkhd->bqhd", window_slopes, window_keys) + einsum_wide(
        "bhqr,rhd->bqhd", global_slopes, global_keys
    )
    query_grads = query_grads.astype(jnp.bfloat16).reshape(block_count, query_count, model_width)
    window_key_grads = einsum_wide("bhqk,bqhd->bkhd", window_slopes, query_heads).reshape(
        block_count, -1, model_width
    )
    window_value_grads = einsum_wide("bhqk,bqhd->bkhd", window_rounded, grad_heads).reshape(
        block_count, -1, model_width
    )
    global_key_grads = einsum_wide("bhqr,bqhd->rhd", global_slopes, query_heads).reshape(
        -1, model_width
    )
    global_value_grads = einsum_wide("bhqr,bqhd->rhd", global_rounded, grad_heads).reshape(
        -1, model_width
    )
    return (
        query_grads,
        jnp.concatenate([window_key_grads, window_value_grads], axis=-1),
        jnp.concatenate([global_key_grads, global_value_grads], axis=-1),
    )


def shards(features, w_query, w_key, w_value, w_out, reg_pos, grad_out):
    tile_rows, tile_cols, model_width = features.shape
    row_count = lax.axis_size("rows")
    col_count = lax.axis_size("cols")
    row_index = lax.axis_index("rows")
    col_index = lax.axis_index("cols")
    first_row = row_index * tile_rows
    first_col = col_index * tile_cols
    row_blocks = tile_rows // BLK
    col_blocks = tile_cols // BLK
    flat_tokens = features.reshape(-1, model_width)
    queries = jnp.dot(flat_tokens, w_query, preferred_element_type=jnp.float32).astype(jnp.bfloat16)
    keys_local = jnp.dot(flat_tokens, w_key, preferred_element_type=jnp.float32).astype(
        jnp.bfloat16
    )
    values_local = jnp.dot(flat_tokens, w_value, preferred_element_type=jnp.float32).astype(
        jnp.bfloat16
    )
    key_value = jnp.concatenate([keys_local, values_local], axis=1)
    framed = with_halo(
        key_value.reshape(tile_rows, tile_cols, 2 * model_width), (("rows", 0), ("cols", 1)), RAD
    )
    row_cells = first_row + jnp.arange(tile_rows, dtype=jnp.int32)
    col_cells = first_col + jnp.arange(tile_cols, dtype=jnp.int32)
    places = (row_cells[:, None] * (tile_cols * col_count) + col_cells[None, :]).reshape(-1)
    own_index = row_index * col_count + col_index
    own_place = lax.dynamic_slice_in_dim(reg_pos, own_index, 1)
    selector = (reg_pos[:, None] == places[None, :]).astype(jnp.bfloat16)
    picked = jnp.dot(selector, key_value, preferred_element_type=jnp.float32)
    global_kv = lax.psum(picked, ("rows", "cols")).astype(jnp.bfloat16)
    window_kv = windows(framed, row_blocks, col_blocks)
    window_mask = block_mask(
        axis_mask(first_row, tile_rows * row_count, row_blocks),
        axis_mask(first_col, tile_cols * col_count, col_blocks),
    )
    query_blocks = to_blocks(
        queries.reshape(tile_rows, tile_cols, model_width), row_blocks, col_blocks
    )
    probs, attended = forward_block(query_blocks, window_kv, global_kv, window_mask)
    attended_flat = from_blocks(attended, row_blocks, col_blocks).reshape(-1, model_width)
    layer_out = (
        jnp.dot(attended_flat, w_out, preferred_element_type=jnp.float32)
        .astype(jnp.bfloat16)
        .reshape(features.shape)
    )
    grad_attended = jnp.dot(
        grad_out.reshape(-1, model_width), w_out.T, preferred_element_type=jnp.float32
    ).astype(jnp.bfloat16)
    grad_blocks = to_blocks(
        grad_attended.reshape(tile_rows, tile_cols, model_width), row_blocks, col_blocks
    )
    query_grads, window_grads, global_grads = backward_block(
        query_blocks, window_kv, global_kv, probs, attended, grad_blocks
    )
    frame_grads = windows_adjoint(window_grads, row_blocks, col_blocks)
    left_rim = frame_grads[:, :RAD]
    right_rim = frame_grads[:, tile_cols + RAD :]
    centre = frame_grads[:, RAD : tile_cols + RAD]
    from_right = from_behind(left_rim.astype(jnp.bfloat16), "cols", -1).astype(left_rim.dtype)
    from_left = from_behind(right_rim.astype(jnp.bfloat16), "cols", 1).astype(right_rim.dtype)
    centre = centre.at[:, tile_cols - RAD :].add(from_right).at[:, :RAD].add(from_left)
    upper_rim = centre[:RAD]
    lower_rim = centre[tile_rows + RAD :]
    middle = centre[RAD : tile_rows + RAD]
    from_below = from_behind(upper_rim.astype(jnp.bfloat16), "rows", -1).astype(upper_rim.dtype)
    from_above = from_behind(lower_rim.astype(jnp.bfloat16), "rows", 1).astype(lower_rim.dtype)
    middle = middle.at[tile_rows - RAD :].add(from_below).at[:RAD].add(from_above)
    summed = lax.psum(global_grads, ("rows", "cols"))
    own_grads = lax.dynamic_slice_in_dim(summed, own_index, 1, 0)
    own_mask = (places == own_place[0])[:, None]
    kv_grads = (middle.reshape(-1, 2 * model_width) + jnp.where(own_mask, own_grads, 0.0)).astype(
        jnp.bfloat16
    )
    query_flat = from_blocks(query_grads, row_blocks, col_blocks).reshape(-1, model_width)
    grad_in = (
        jnp.dot(query_flat, w_query.T, preferred_element_type=jnp.float32)
        + jnp.dot(kv_grads[:, :model_width], w_key.T, preferred_element_type=jnp.float32)
        + jnp.dot(kv_grads[:, model_width:], w_value.T, preferred_element_type=jnp.float32)
    )
    grad_in = grad_in.astype(jnp.bfloat16).reshape(features.shape)
    return (layer_out, grad_in)


def solution(mesh):
    placed = (P("rows", "cols", None), P(), P(), P(), P(), P(), P("rows", "cols", None))
    return jax.shard_map(
        shards,
        mesh=mesh,
        in_specs=placed,
        out_specs=(P("rows", "cols", None), P("rows", "cols", None)),
        check_vma=False,
    )
```

profile of v0, /device:TPU:4, one launch (start us, length us, event | category | flops | bytes accessed | tf_op | source)
XLA Modules:
  0.0 399.4 jit_solution(14206506281566383169)
XLA Ops:
  12.8 3.4 collective-permute-start
  17.2 3.3 collective-permute-start.1
  22.6 53.4 %all-reduce.4 = bf16[32,2048]{1,0:T(8,128)(2,1)S(1)} all-reduce(f32[32,2048]{1,0:T(8,128)S(1)} %fusion.38), channel_id=1, replica_groups=mesh['rows'=4,'cols'=8] {'rows','cols'}, use_global_device_ids=true, to_apply=%region_1.2 | all-reduce | flops 65536 | bytes 393216 | tf_op jit(solution)/shard_map/psum | solution.py:209
  100.9 3.6 pad_maximum_fusion.1
  104.5 4.4 %gather_fusion = bf16[2,20,20,2048]{3,1,2,0:T(8,128)(2,1)} fusion(bf16[20,28,2048]{2,0,1:T(8,128)(2,1)} %pad_maximum_fusion.1, s32[2]{0:T(128)S(1)} %fusion.46), kind=kCustom, calls=%fused_computation | custom fusion | bytes 6553624 | tf_op jit(solution)/shard_map/vmap()/gather | solution.py:70
  109.0 5.5 %copy.135 = bf16[2,20,20,2048]{3,0,2,1:T(2,128)(2,1)S(1)} copy(bf16[2,20,20,2048]{3,1,2,0:T(8,128)(2,1)} %gather_fusion) | data formatting | bytes 6553600 | tf_op jit(solution)/shard_map/vmap()/gather | solution.py:70
  114.4 3.5 fusion.53
  118.0 6.0 %copy.136 = bf16[2,400,1024]{1,2,0:T(8,128)(2,1)} copy(bf16[2,400,1024]{2,0,1:T(2,128)(2,1)} %get-tuple-element.146) | data formatting | bytes 3276800 | tf_op jit(solution)/shard_map/slice | solution.py:103
  124.0 6.0 %copy.138 = bf16[2,400,1024]{1,2,0:T(8,128)(2,1)} copy(bf16[2,400,1024]{2,0,1:T(2,128)(2,1)} %get-tuple-element.147) | data formatting | bytes 3276800 | tf_op jit(solution)/shard_map/slice | solution.py:102
  147.0 5.4 %copy.162 = f32[2,400,1024]{2,1,0:T(8,128)} copy(f32[2,400,1024]{1,2,0:T(8,128)} %bitcast.124) | data formatting | bytes 6553600 | tf_op jit(solution)/shard_map/reshape | solution.py:164
  152.3 4.2 %fusion.59 = f32[2,16,64,400]{3,2,1,0:T(8,128)} fusion(bf16[2,64,16,64]{1,3,2,0:T(8,128)(2,1)S(1)} %copy-done.7, bf16[2,16,64,400]{3,2,1,0:T(8,128)(2,1)} %multiply_convert_fusion), kind=kOutput, calls=%fused_computation.125 | convolution fusion | flops 104857600 | bytes 5177344 | tf_op jit(solution)/shard_map/bhqk,bqhd->bkhd/dot_general | solution.py:110
  156.6 5.2 %copy.161 = f32[2,400,1024]{2,1,0:T(8,128)} copy(f32[2,400,1024]{1,2,0:T(8,128)} %bitcast.122) | data formatting | bytes 6553600 | tf_op jit(solution)/shard_map/reshape | solution.py:161
  161.8 6.5 %pad_maximum_fusion = f32[2,400,2048]{2,1,0:T(8,128)} fusion(f32[2,400,1024]{2,1,0:T(8,128)} %copy.162, f32[2,400,1024]{2,1,0:T(8,128)} %copy.161), kind=kLoop, calls=%fused_computation.3 | loop fusion | flops 1638400 | bytes 13107200 | tf_op jit(solution)/shard_map/concatenate | solution.py:175
  171.2 59.6 %while.19 = (s32[]{:T(128)}, f32[20,28,2048]{2,1,0:T(8,128)}, f32[2,400,2048]{2,1,0:T(8,128)}, s32[]{:T(128)}, s32[]{:T(128)}, /*index=5*/s32[]{:T(128)}, s32[]{:T(128)}, s32[]{:T(128)}) while((s32[]{:T(128)}, f32[20,28,2048]{2,1,0:T(8,128)}, f32[2,400,2048]{2,1,0:T(8,128)}, s32[]{:T(128)}, s32[]{:T(128)}, /*index=5*/s32[]{:T(128)}, ...), condition=%wide.region_6.7_spmd, body=%wide.region_5.6_spmd.sunk | while | flops 819212 | bytes 29491408 | solution.py:95
  171.3 4.0 %constant_dynamic-slice_fusion.3 = f32[1,400,2048]{2,1,0:T(8,128)} fusion(f32[2,400,2048]{2,1,0:T(8,128)} %get-tuple-element.207, s32[]{:T(128)S(6)} %copy.226), kind=kLoop, calls=%fused_computation.2.clone.1 | loop fusion | bytes 6553604 | tf_op jit(solution)/shard_map/while/body/eval_jaxpr/jit(dynamic_index_in_dim)/dynamic_slice | solution.py:89
  175.3 4.6 %reshape.534 = f32[20,20,2048]{2,1,0:T(8,128)} reshape(f32[1,400,2048]{2,1,0:T(8,128)} %constant_dynamic-slice_fusion.3) | data formatting | bytes 6553600 | tf_op jit(solution)/shard_map/while/body/eval_jaxpr/reshape | solution.py:89
  179.8 6.9 %dynamic-slice_add_fusion.2 = f32[20,20,2048]{2,1,0:T(8,128)} fusion(f32[20,20,2048]{2,1,0:T(8,128)} %reshape.534, f32[20,28,2048]{2,1,0:T(8,128)} %get-tuple-element.198, s32[]{:T(128)S(6)} %select_n.177), kind=kLoop, calls=%fused_computation.1.clone.1 | loop fusion | flops 819200 | bytes 9830404 | tf_op jit(solution)/shard_map/while/body/eval_jaxpr/add | solution.py:93
  186.8 14.7 %dynamic_update_slice.12 = f32[20,28,2048]{2,1,0:T(8,128)} dynamic-update-slice(f32[20,28,2048]{2,1,0:T(8,128)} %get-tuple-element.198, f32[20,20,2048]{2,1,0:T(8,128)} %dynamic-slice_add_fusion.2, s32[]{:T(128)} %constant.262.clone.1..sunk, s32[]{:T(128)S(6)} %select_n.177, s32[]{:T(128)} %constant.262.clone.1..sunk) | dynamic-update-slice | bytes 6553604 | tf_op jit(solution)/shard_map/while/body/eval_jaxpr/dynamic_update_slice | solution.py:93
  201.5 4.0 %constant_dynamic-slice_fusion.3 = f32[1,400,2048]{2,1,0:T(8,128)} fusion(f32[2,400,2048]{2,1,0:T(8,128)} %get-tuple-element.207, s32[]{:T(128)S(6)} %copy.226), kind=kLoop, calls=%fused_computation.2.clone.1 | loop fusion | bytes 6553604 | tf_op jit(solution)/shard_map/while/body/eval_jaxpr/jit(dynamic_index_in_dim)/dynamic_slice | solution.py:89
  205.5 4.6 %reshape.534 = f32[20,20,2048]{2,1,0:T(8,128)} reshape(f32[1,400,2048]{2,1,0:T(8,128)} %constant_dynamic-slice_fusion.3) | data formatting | bytes 6553600 | tf_op jit(solution)/shard_map/while/body/eval_jaxpr/reshape | solution.py:89
  210.1 6.6 %dynamic-slice_add_fusion.2 = f32[20,20,2048]{2,1,0:T(8,128)} fusion(f32[20,20,2048]{2,1,0:T(8,128)} %reshape.534, f32[20,28,2048]{2,1,0:T(8,128)} %get-tuple-element.198, s32[]{:T(128)S(6)} %select_n.177), kind=kLoop, calls=%fused_computation.1.clone.1 | loop fusion | flops 819200 | bytes 9830404 | tf_op jit(solution)/shard_map/while/body/eval_jaxpr/add | solution.py:93
  216.6 14.2 %dynamic_update_slice.12 = f32[20,28,2048]{2,1,0:T(8,128)} dynamic-update-slice(f32[20,28,2048]{2,1,0:T(8,128)} %get-tuple-element.198, f32[20,20,2048]{2,1,0:T(8,128)} %dynamic-slice_add_fusion.2, s32[]{:T(128)} %constant.262.clone.1..sunk, s32[]{:T(128)S(6)} %select_n.177, s32[]{:T(128)} %constant.262.clone.1..sunk) | dynamic-update-slice | bytes 6553604 | tf_op jit(solution)/shard_map/while/body/eval_jaxpr/dynamic_update_slice | solution.py:93
  230.8 4.3 %slice.170 = f32[20,16,2048]{2,1,0:T(8,128)} slice(f32[20,28,2048]{2,1,0:T(8,128)} %get-tuple-element.139), slice={[0:20], [6:22], [0:2048]} | slice | bytes 5242880 | tf_op jit(solution)/shard_map/slice | solution.py:237
  235.1 4.0 %copy.215 = bf16[20,28,2048]{2,0,1:T(8,128)(2,1)} copy(f32[20,28,2048]{2,1,0:T(8,128)S(1)} %copy-done.1) | data formatting | bytes 6881280 | tf_op jit(solution)/shard_map/while | solution.py:95
  251.3 3.1 fusion.6
  256.3 4.5 %collective-permute-start.5 = (bf16[20,6,2048]{2,0,1:T(8,128)(2,1)}, bf16[20,6,2048]{2,0,1:T(8,128)(2,1)}, u32[]{:S(2)}, u32[]{:S(2)}) collective-permute-start(bf16[20,6,2048]{2,0,1:T(8,128)(2,1)} %get-tuple-element.148), channel_id=1, source_target_pairs={{0,1},{1,2},{2,3},{3,4},{4,5},{5,6},{6,7},{8,9},{9,10},{10,11},{11... | collective-permute-start | bytes 1474568 | tf_op jit(solution)/shard_map/ppermute | solution.py:29
  264.3 6.2 %scatter-add.14 = f32[20,16,2048]{2,1,0:T(8,128)} dynamic-update-slice(f32[20,16,2048]{2,1,0:T(8,128)} %slice.170, f32[20,6,2048]{2,1,0:T(8,128)S(1)} %convert_add_fusion, s32[]{:T(128)} %constant.262.clone.1, s32[]{:T(128)} %constant.280.clone.1, s32[]{:T(128)} %constant.262.clone.1) | dynamic-update-slice | bytes 1966084 | tf_op jit(solution)/shard_map/scatter-add | solution.py:240
  272.3 7.0 %scatter-add.15 = f32[20,16,2048]{2,1,0:T(8,128)} dynamic-update-slice(f32[20,16,2048]{2,1,0:T(8,128)} %scatter-add.14, f32[20,6,2048]{2,1,0:T(8,128)S(1)} %slice_add_fusion, s32[]{:T(128)} %constant.262.clone.1, s32[]{:T(128)} %constant.262.clone.1, s32[]{:T(128)} %constant.262.clone.1) | dynamic-update-slice | bytes 1966084 | tf_op jit(solution)/shard_map/scatter-add | solution.py:240
  281.5 3.3 collective-permute-start.6
  286.0 88.5 %all-reduce.3.cloned.1.call-done = f32[32,2048]{1,0:T(8,128)} async-done(((f32[32,2048]{1,0:T(8,128)}), f32[32,2048]{1,0:T(8,128)}) %all-reduce.3.cloned.1.call-update) | async-done | bytes 262160 | tf_op jit(solution)/shard_map/psum | solution.py:247
  376.7 3.5 collective-permute-start.7
  381.5 8.3 %collective-permute-done.7 = bf16[6,16,2048]{2,1,0:T(8,128)(2,1)S(1)} collective-permute-done((bf16[6,16,2048]{2,1,0:T(8,128)(2,1)S(1)}, bf16[6,16,2048]{2,1,0:T(8,128)(2,1)S(1)}, u32[]{:S(2)}, u32[]{:S(2)}) %collective-permute-start.7) | collective-permute-done | bytes 393248 | tf_op jit(solution)/shard_map/ppermute | solution.py:29
  (138 shorter events, 81.8 us)
Async XLA Ops:
  7.2 74.9 %copy-start = (bf16[1024,1024]{1,0:T(8,128)(2,1)S(1)}, bf16[1024,1024]{1,0:T(8,128)(2,1)}, u32[]{:S(2)}) copy-start(bf16[1024,1024]{1,0:T(8,128)(2,1)} %param.18) | copy-start | bytes 6291460
  7.2 367.4 %all-reduce.3.cloned.1.call-start = ((), (), s32[]{:S(2)}) async-start(), calls=%async_computation | async-start | bytes 524288 | tf_op jit(solution)/shard_map/psum | solution.py:247
  9.5 12.3 %copy-start.20 = (s32[32]{0:T(128)S(1)}, s32[32]{0:T(128)}, u32[]{:S(2)}) copy-start(s32[32]{0:T(128)} %param.22) | copy-start | bytes 388
  11.6 64.4 %copy-start.17 = (bf16[8,16,1024]{2,1,0:T(8,128)(2,1)S(1)}, bf16[8,16,1024]{2,1,0:T(8,128)(2,1)}, u32[]{:S(2)}) copy-start(bf16[8,16,1024]{2,1,0:T(8,128)(2,1)} %param.23) | copy-start | bytes 786436
  12.8 69.8 %collective-permute-start = (bf16[6,16,2048]{2,0,1:T(8,128)(2,1)}, bf16[6,16,2048]{2,0,1:T(8,128)(2,1)}, u32[]{:S(2)}, u32[]{:S(2)}) collective-permute-start(bf16[6,16,2048]{2,0,1:T(8,128)(2,1)} %copy.132), channel_id=1, source_target_pairs={{0,8},{8,16},{16,24},{1,9},{9,17},{17,25},{2,10},{10,18},{18,26},{... | collective-permute-start | bytes 1179656 | tf_op jit(solution)/shard_map/ppermute | solution.py:18
  17.2 65.4 %collective-permute-start.1 = (bf16[6,16,2048]{2,0,1:T(8,128)(2,1)}, bf16[6,16,2048]{2,0,1:T(8,128)(2,1)}, u32[]{:S(2)}, u32[]{:S(2)}) collective-permute-start(bf16[6,16,2048]{2,0,1:T(8,128)(2,1)} %copy.133), channel_id=1, source_target_pairs={{8,0},{16,8},{24,16},{9,1},{17,9},{25,17},{10,2},{18,10},{26,18},{... | collective-permute-start | bytes 1179656 | tf_op jit(solution)/shard_map/ppermute | solution.py:21
  76.0 6.1 %copy-start.9 = (bf16[8,16,1024]{2,1,0:T(8,128)(2,1)S(1)}, bf16[8,16,1024]{2,1,0:T(8,128)(2,1)}, u32[]{:S(2)}) copy-start(bf16[8,16,1024]{2,1,0:T(8,128)(2,1)} %param.17) | copy-start | bytes 786436
  82.1 0.8 copy-start.6
  85.6 15.3 %collective-permute-start.2 = (bf16[20,6,2048]{2,0,1:T(8,128)(2,1)}, bf16[20,6,2048]{2,0,1:T(8,128)(2,1)}, u32[]{:S(2)}, u32[]{:S(2)}) collective-permute-start(bf16[20,6,2048]{2,0,1:T(8,128)(2,1)} %get-tuple-element.150), channel_id=1, source_target_pairs={{0,1},{1,2},{2,3},{3,4},{4,5},{5,6},{6,7},{8,9},{9,10},{10,11},{11... | collective-permute-start | bytes 1474568 | tf_op jit(solution)/shard_map/ppermute | solution.py:18
  87.8 13.1 %collective-permute-start.3 = (bf16[20,6,2048]{2,0,1:T(8,128)(2,1)}, bf16[20,6,2048]{2,0,1:T(8,128)(2,1)}, u32[]{:S(2)}, u32[]{:S(2)}) collective-permute-start(bf16[20,6,2048]{2,0,1:T(8,128)(2,1)} %get-tuple-element.151), channel_id=1, source_target_pairs={{1,0},{2,1},{3,2},{4,3},{5,4},{6,5},{7,6},{9,8},{10,9},{11,10},{12... | collective-permute-start | bytes 1474568 | tf_op jit(solution)/shard_map/ppermute | solution.py:21
  94.7 4.8 %copy-start.13 = (bf16[32,16,64]{2,1,0:T(8,128)(2,1)S(1)}, bf16[32,16,64]{2,1,0:T(8,128)(2,1)}, u32[]{:S(2)}) copy-start(bf16[32,16,64]{2,1,0:T(8,128)(2,1)} %reshape.508) | copy-start | bytes 196612
  132.8 1.2 copy-start.11
  132.8 2.4 copy-start.19
  134.0 1.6 copy-start.16
  135.6 3.1 copy-start.10
  135.6 3.1 copy-start.15
  147.0 5.4 %copy-start.7 = (bf16[2,64,16,64]{1,3,2,0:T(8,128)(2,1)S(1)}, bf16[2,64,16,64]{1,3,2,0:T(8,128)(2,1)}, u32[]{:S(2)}) copy-start(bf16[2,64,16,64]{1,3,2,0:T(8,128)(2,1)} %copy.159) | copy-start | bytes 786436
  230.8 4.3 %copy-start.1 = (f32[20,28,2048]{2,1,0:T(8,128)S(1)}, f32[20,28,2048]{2,1,0:T(8,128)}, u32[]{:S(2)}) copy-start(f32[20,28,2048]{2,1,0:T(8,128)} %get-tuple-element.139) | copy-start | bytes 13762564
  235.1 4.0 %copy-start.18 = (f32[32,16,64]{2,0,1:T(8,128)S(1)}, f32[32,16,64]{2,0,1:T(8,128)}, u32[]{:S(2)}) copy-start(f32[32,16,64]{2,0,1:T(8,128)} %convolution_bitcast_fusion.5) | copy-start | bytes 393220
  239.4 11.9 %copy-start.8 = (f32[2,64,16,64]{1,3,2,0:T(8,128)S(1)}, f32[2,64,16,64]{1,3,2,0:T(8,128)}, u32[]{:S(2)}) copy-start(f32[2,64,16,64]{1,3,2,0:T(8,128)} %convolution_bitcast_fusion) | copy-start | bytes 1572868
  247.5 3.9 copy-start.2
  250.0 12.4 %collective-permute-start.4 = (bf16[20,6,2048]{2,0,1:T(8,128)(2,1)}, bf16[20,6,2048]{2,0,1:T(8,128)(2,1)}, u32[]{:S(2)}, u32[]{:S(2)}) collective-permute-start(bf16[20,6,2048]{2,0,1:T(8,128)(2,1)} %get-tuple-element.149), channel_id=1, source_target_pairs={{1,0},{2,1},{3,2},{4,3},{5,4},{6,5},{7,6},{9,8},{10,9},{11,10},{12... | collective-permute-start | bytes 1474568 | tf_op jit(solution)/shard_map/ppermute | solution.py:29
  256.3 14.2 %collective-permute-start.5 = (bf16[20,6,2048]{2,0,1:T(8,128)(2,1)}, bf16[20,6,2048]{2,0,1:T(8,128)(2,1)}, u32[]{:S(2)}, u32[]{:S(2)}) collective-permute-start(bf16[20,6,2048]{2,0,1:T(8,128)(2,1)} %get-tuple-element.148), channel_id=1, source_target_pairs={{0,1},{1,2},{2,3},{3,4},{4,5},{5,6},{6,7},{8,9},{9,10},{10,11},{11... | collective-permute-start | bytes 1474568 | tf_op jit(solution)/shard_map/ppermute | solution.py:29
  279.4 5.5 %copy-start.3 = (bf16[1024,1024]{1,0:T(8,128)(2,1)S(1)}, bf16[1024,1024]{1,0:T(8,128)(2,1)}, u32[]{:S(2)}) copy-start(bf16[1024,1024]{1,0:T(8,128)(2,1)} %param.21) | copy-start | bytes 6291460
  279.4 5.5 %copy-start.14 = (bf16[1,8,2,8,1024]{4,3,2,1,0:T(8,128)(2,1)S(1)}, bf16[1,8,2,8,1024]{4,3,2,1,0:T(8,128)(2,1)}, u32[]{:S(2)}) copy-start(bf16[1,8,2,8,1024]{4,3,2,1,0:T(8,128)(2,1)} %copy.149) | copy-start | bytes 786436
  281.5 98.7 %collective-permute-start.6 = (bf16[6,16,2048]{2,1,0:T(8,128)(2,1)S(1)}, bf16[6,16,2048]{2,1,0:T(8,128)(2,1)S(1)}, u32[]{:S(2)}, u32[]{:S(2)}) collective-permute-start(bf16[6,16,2048]{2,1,0:T(8,128)(2,1)S(1)} %get-tuple-element.153), channel_id=1, source_target_pairs={{8,0},{16,8},{24,16},{9,1},{17,9},{25,17},{10,2},{18,10},{26,18},{... | collective-permute-start | bytes 1179656 | tf_op jit(solution)/shard_map/ppermute | solution.py:29
  376.7 13.4 %copy-start.5 = (bf16[1024,1024]{1,0:T(8,128)(2,1)S(1)}, bf16[1024,1024]{1,0:T(8,128)(2,1)}, u32[]{:S(2)}) copy-start(bf16[1024,1024]{1,0:T(8,128)(2,1)} %param.19) | copy-start | bytes 6291460
  376.7 13.4 %copy-start.12 = (f32[128,1024]{1,0:T(8,128)S(1)}, f32[128,1024]{1,0:T(8,128)}, u32[]{:S(2)}) copy-start(f32[128,1024]{1,0:T(8,128)} %fusion.58) | copy-start | bytes 1572868
  376.7 13.0 %collective-permute-start.7 = (bf16[6,16,2048]{2,1,0:T(8,128)(2,1)S(1)}, bf16[6,16,2048]{2,1,0:T(8,128)(2,1)S(1)}, u32[]{:S(2)}, u32[]{:S(2)}) collective-permute-start(bf16[6,16,2048]{2,1,0:T(8,128)(2,1)S(1)} %get-tuple-element.152), channel_id=1, source_target_pairs={{0,8},{8,16},{16,24},{1,9},{9,17},{17,25},{2,10},{10,18},{18,26},{... | collective-permute-start | bytes 1179656 | tf_op jit(solution)/shard_map/ppermute | solution.py:29
  381.5 9.5 %copy-start.4 = (bf16[1024,1024]{1,0:T(8,128)(2,1)S(1)}, bf16[1024,1024]{1,0:T(8,128)(2,1)}, u32[]{:S(2)}) copy-start(bf16[1024,1024]{1,0:T(8,128)(2,1)} %param.20) | copy-start | bytes 6291460
Sparse Core Ops, SparseCore 0:
  247.6 126.9 all-reduce.2
where the time goes:
time: 402 us; the launch traced here: 399 us
  local copies, waits for them, and re-layouts  134 us (33%)
  waiting for transfers between devices  96.8 us (24%)
  blocking collectives  53.4 us (13%)
  other arithmetic  40.4 us (10%)
  matrix products  36.9 us (9%)
  starting transfers between devices  22.9 us (6%)
  between operations  14.7 us (4%)
    psum x1, waiting for transfers between devices, shards(): summed = lax.psum(global_grads, ('rows', 'cols'))  88.5 us
    psum x1, blocking collectives, shards(): global_kv = lax.psum(picked, ('rows', 'cols')).astype(jnp.bfloat16)  53.4 us
    dynamic_update_slice x2, local copies, waits for them, and re-layouts, add_box(): return lax.dynamic_update_slice(accum, current + piece, start)  28.9 us
    dot_general x12, matrix products, einsum_wide(): return jnp.einsum(form, left, right, preferred_element_type=jnp.float32)  24.2 us
    add x2, other arithmetic, add_box(): return lax.dynamic_update_slice(accum, current + piece, start)  13.5 us
    scatter-add x2, local copies, waits for them, and re-layouts, shards(): centre.at[:, tile_cols - RAD:].add(from_right).at[:, :RAD].add(from_left)  13.3 us
    ppermute x4, starting transfers between devices, from_behind(): return lax.ppermute(x, axis, pairs)  12.6 us
    gather x2, local copies, waits for them, and re-layouts, cut_box(): lax.dynamic_slice(framed, (top_cell, left_cell, jnp.int32(0)), (span_cell...  9.92 us
  transfers between devices with their start and end apart: 9, of which 2 were waited for; matrix products, arithmetic and copies ran while one was open for 14% of the time, Pallas kernels for 0%

commit v1 on v0

--- a/solution.py
+++ b/solution.py
@@ -244,7 +244,7 @@
     from_below = from_behind(upper_rim.astype(jnp.bfloat16), "rows", -1).astype(upper_rim.dtype)
     from_above = from_behind(lower_rim.astype(jnp.bfloat16), "rows", 1).astype(lower_rim.dtype)
     middle = middle.at[tile_rows - RAD :].add(from_below).at[:RAD].add(from_above)
-    summed = lax.psum(global_grads, ("rows", "cols"))
+    summed = lax.psum(lax.psum(global_grads, "cols"), "rows")
     own_grads = lax.dynamic_slice_in_dim(summed, own_index, 1, 0)
     own_mask = (places == own_place[0])[:, None]
     kv_grads = (middle.reshape(-1, 2 * model_width) + jnp.where(own_mask, own_grads, 0.0)).astype(

time: 402 us -> 324 us (0.81)
  waiting for transfers between devices: 96.8 us -> 30.1 us
  local copies, waits for them, and re-layouts: 134 us -> 129 us
    psum x1 -> x2, waiting for transfers between devices: 88.5 us -> 20.7 us  [shards(): summed = lax.psum(lax.psum(global_grads, 'cols'), 'rows')]
  transfers between devices with their start and end apart: 9 -> 10, of which waited for: 2 -> 2; matrix products, arithmetic and copies ran while one was open for 14% -> 43% of each run, Pallas kernels for 0% -> 0%
where the time goes in v1:
time: 324 us; the launch traced here: 321 us
  local copies, waits for them, and re-layouts  129 us (40%)
  blocking collectives  53.4 us (16%)
  other arithmetic  39.5 us (12%)
  matrix products  33.1 us (10%)
  waiting for transfers between devices  30.1 us (9%)
  starting transfers between devices  22 us (7%)
  between operations  14.7 us (5%)
    psum x1, blocking collectives, shards(): global_kv = lax.psum(picked, ('rows', 'cols')).astype(jnp.bfloat16)  53.4 us
    dynamic_update_slice x2, local copies, waits for them, and re-layouts, add_box(): return lax.dynamic_update_slice(accum, current + piece, start)  28.9 us
    psum x2, waiting for transfers between devices, shards(): summed = lax.psum(lax.psum(global_grads, 'cols'), 'rows')  20.7 us
    dot_general x12, matrix products, einsum_wide(): return jnp.einsum(form, left, right, preferred_element_type=jnp.float32)  20.4 us
    add x2, other arithmetic, add_box(): return lax.dynamic_update_slice(accum, current + piece, start)  13.5 us
    scatter-add x2, local copies, waits for them, and re-layouts, shards(): centre.at[:, tile_cols - RAD:].add(from_right).at[:, :RAD].add(from_left)  13.2 us
    ppermute x4, starting transfers between devices, from_behind(): return lax.ppermute(x, axis, pairs)  11.8 us
    gather x2, local copies, waits for them, and re-layouts, cut_box(): lax.dynamic_slice(framed, (top_cell, left_cell, jnp.int32(0)), (span_cell...  9.92 us
  transfers between devices with their start and end apart: 10, of which 2 were waited for; matrix products, arithmetic and copies ran while one was open for 43% of the time, Pallas kernels for 0%

profile of v1, /device:TPU:4, one launch (start us, length us, event | category | flops | bytes accessed | tf_op | source)
XLA Modules:
  0.0 321.4 jit_solution(4934521589643183142)
XLA Ops:
  12.8 3.4 %collective-permute-start = (bf16[6,16,2048]{2,0,1:T(8,128)(2,1)}, bf16[6,16,2048]{2,0,1:T(8,128)(2,1)}, u32[]{:S(2)}, u32[]{:S(2)}) collective-permute-start(bf16[6,16,2048]{2,0,1:T(8,128)(2,1)} %copy.132), channel_id=1, source_target_pairs={{0,8},{8,16},{16,24},{1,9},{9,17},{17,25},{2,10},{10,18},{18,26},{... | collective-permute-start | bytes 1179656 | tf_op jit(solution)/shard_map/ppermute | solution.py:18
  17.2 3.3 %collective-permute-start.1 = (bf16[6,16,2048]{2,0,1:T(8,128)(2,1)}, bf16[6,16,2048]{2,0,1:T(8,128)(2,1)}, u32[]{:S(2)}, u32[]{:S(2)}) collective-permute-start(bf16[6,16,2048]{2,0,1:T(8,128)(2,1)} %copy.133), channel_id=1, source_target_pairs={{8,0},{16,8},{24,16},{9,1},{17,9},{25,17},{10,2},{18,10},{26,18},{... | collective-permute-start | bytes 1179656 | tf_op jit(solution)/shard_map/ppermute | solution.py:21
  22.6 53.4 %all-reduce.7 = bf16[32,2048]{1,0:T(8,128)(2,1)S(1)} all-reduce(f32[32,2048]{1,0:T(8,128)S(1)} %fusion.38), channel_id=1, replica_groups=mesh['rows'=4,'cols'=8] {'rows','cols'}, use_global_device_ids=true, to_apply=%region_1.2 | all-reduce | flops 65536 | bytes 393216 | tf_op jit(solution)/shard_map/psum | solution.py:209
  100.9 3.6 %pad_maximum_fusion.1 = bf16[20,28,2048]{2,0,1:T(8,128)(2,1)} fusion(bf16[20,6,2048]{2,0,1:T(8,128)(2,1)} %collective-permute-done.3, bf16[6,16,2048]{2,0,1:T(8,128)(2,1)} %collective-permute-done.1, bf16[8,16,2048]{2,0,1:T(8,128)(2,1)} %copy-done.6, bf16[6,16,2048]{2,0,1:T(8,128)(2,1)} %collective-permute-done, bf16[20,6,2048]{2,0,1:T(8,128)(2,1)} %collective-permute-done.2), kind=kLoop, calls=%fused_computation.11 | loop fusion | flops 11468800 | bytes 4587520 | tf_op jit(solution)/shard_map/concatenate | solution.py:22
  104.5 4.4 %gather_fusion = bf16[2,20,20,2048]{3,1,2,0:T(8,128)(2,1)} fusion(bf16[20,28,2048]{2,0,1:T(8,128)(2,1)} %pad_maximum_fusion.1, s32[2]{0:T(128)S(1)} %fusion.46), kind=kCustom, calls=%fused_computation | custom fusion | bytes 6553624 | tf_op jit(solution)/shard_map/vmap()/gather | solution.py:70
  109.0 5.5 %copy.135 = bf16[2,20,20,2048]{3,0,2,1:T(2,128)(2,1)S(1)} copy(bf16[2,20,20,2048]{3,1,2,0:T(8,128)(2,1)} %gather_fusion) | data formatting | bytes 6553600 | tf_op jit(solution)/shard_map/vmap()/gather | solution.py:70
  114.5 3.5 %fusion.53 = (bf16[2,400,1024]{2,0,1:T(2,128)(2,1)}, bf16[2,400,1024]{2,0,1:T(2,128)(2,1)}) fusion(bf16[2,400,2048]{2,0,1:T(2,128)(2,1)S(1)} %bitcast.123), kind=kLoop, calls=%fused_computation.119 | loop fusion | bytes 6553600 | tf_op jit(solution)/shard_map/slice | solution.py:103
  118.0 6.0 %copy.136 = bf16[2,400,1024]{1,2,0:T(8,128)(2,1)} copy(bf16[2,400,1024]{2,0,1:T(2,128)(2,1)} %get-tuple-element.146) | data formatting | bytes 3276800 | tf_op jit(solution)/shard_map/slice | solution.py:103
  124.0 6.0 %copy.138 = bf16[2,400,1024]{1,2,0:T(8,128)(2,1)} copy(bf16[2,400,1024]{2,0,1:T(2,128)(2,1)} %get-tuple-element.147) | data formatting | bytes 3276800 | tf_op jit(solution)/shard_map/slice | solution.py:102
  135.0 3.0 fusion.14
  146.0 5.5 %copy.162 = f32[2,400,1024]{2,1,0:T(8,128)} copy(f32[2,400,1024]{1,2,0:T(8,128)} %bitcast.124) | data formatting | bytes 6553600 | tf_op jit(solution)/shard_map/reshape | solution.py:164
  152.6 4.2 %fusion.59 = f32[2,16,64,400]{3,2,1,0:T(8,128)} fusion(bf16[2,64,16,64]{1,3,2,0:T(8,128)(2,1)S(1)} %copy-done.7, bf16[2,16,64,400]{3,2,1,0:T(8,128)(2,1)} %multiply_convert_fusion), kind=kOutput, calls=%fused_computation.125 | convolution fusion | flops 104857600 | bytes 5177344 | tf_op jit(solution)/shard_map/bhqk,bqhd->bkhd/dot_general | solution.py:110
  156.8 5.3 %copy.161 = f32[2,400,1024]{2,1,0:T(8,128)} copy(f32[2,400,1024]{1,2,0:T(8,128)} %bitcast.122) | data formatting | bytes 6553600 | tf_op jit(solution)/shard_map/reshape | solution.py:161
  162.1 6.5 %pad_maximum_fusion = f32[2,400,2048]{2,1,0:T(8,128)} fusion(f32[2,400,1024]{2,1,0:T(8,128)} %copy.162, f32[2,400,1024]{2,1,0:T(8,128)} %copy.161), kind=kLoop, calls=%fused_computation.3 | loop fusion | flops 1638400 | bytes 13107200 | tf_op jit(solution)/shard_map/concatenate | solution.py:175
  168.6 3.0 broadcast_in_dim.31
  171.6 59.6 %while.19 = (s32[]{:T(128)}, f32[20,28,2048]{2,1,0:T(8,128)}, f32[2,400,2048]{2,1,0:T(8,128)}, s32[]{:T(128)}, s32[]{:T(128)}, /*index=5*/s32[]{:T(128)}, s32[]{:T(128)}, s32[]{:T(128)}) while((s32[]{:T(128)}, f32[20,28,2048]{2,1,0:T(8,128)}, f32[2,400,2048]{2,1,0:T(8,128)}, s32[]{:T(128)}, s32[]{:T(128)}, /*index=5*/s32[]{:T(128)}, ...), condition=%wide.region_6.7_spmd, body=%wide.region_5.6_spmd.sunk | while | flops 819212 | bytes 29491408 | solution.py:95
  171.6 4.0 %constant_dynamic-slice_fusion.3 = f32[1,400,2048]{2,1,0:T(8,128)} fusion(f32[2,400,2048]{2,1,0:T(8,128)} %get-tuple-element.207, s32[]{:T(128)S(6)} %copy.226), kind=kLoop, calls=%fused_computation.2.clone.1 | loop fusion | bytes 6553604 | tf_op jit(solution)/shard_map/while/body/eval_jaxpr/jit(dynamic_index_in_dim)/dynamic_slice | solution.py:89
  175.6 4.6 %reshape.534 = f32[20,20,2048]{2,1,0:T(8,128)} reshape(f32[1,400,2048]{2,1,0:T(8,128)} %constant_dynamic-slice_fusion.3) | data formatting | bytes 6553600 | tf_op jit(solution)/shard_map/while/body/eval_jaxpr/reshape | solution.py:89
  180.2 6.9 %dynamic-slice_add_fusion.2 = f32[20,20,2048]{2,1,0:T(8,128)} fusion(f32[20,20,2048]{2,1,0:T(8,128)} %reshape.534, f32[20,28,2048]{2,1,0:T(8,128)} %get-tuple-element.198, s32[]{:T(128)S(6)} %select_n.177), kind=kLoop, calls=%fused_computation.1.clone.1 | loop fusion | flops 819200 | bytes 9830404 | tf_op jit(solution)/shard_map/while/body/eval_jaxpr/add | solution.py:93
  187.2 14.7 %dynamic_update_slice.12 = f32[20,28,2048]{2,1,0:T(8,128)} dynamic-update-slice(f32[20,28,2048]{2,1,0:T(8,128)} %get-tuple-element.198, f32[20,20,2048]{2,1,0:T(8,128)} %dynamic-slice_add_fusion.2, s32[]{:T(128)} %constant.262.clone.1..sunk, s32[]{:T(128)S(6)} %select_n.177, s32[]{:T(128)} %constant.262.clone.1..sunk) | dynamic-update-slice | bytes 6553604 | tf_op jit(solution)/shard_map/while/body/eval_jaxpr/dynamic_update_slice | solution.py:93
  201.9 4.0 %constant_dynamic-slice_fusion.3 = f32[1,400,2048]{2,1,0:T(8,128)} fusion(f32[2,400,2048]{2,1,0:T(8,128)} %get-tuple-element.207, s32[]{:T(128)S(6)} %copy.226), kind=kLoop, calls=%fused_computation.2.clone.1 | loop fusion | bytes 6553604 | tf_op jit(solution)/shard_map/while/body/eval_jaxpr/jit(dynamic_index_in_dim)/dynamic_slice | solution.py:89
  205.9 4.6 %reshape.534 = f32[20,20,2048]{2,1,0:T(8,128)} reshape(f32[1,400,2048]{2,1,0:T(8,128)} %constant_dynamic-slice_fusion.3) | data formatting | bytes 6553600 | tf_op jit(solution)/shard_map/while/body/eval_jaxpr/reshape | solution.py:89
  210.5 6.6 %dynamic-slice_add_fusion.2 = f32[20,20,2048]{2,1,0:T(8,128)} fusion(f32[20,20,2048]{2,1,0:T(8,128)} %reshape.534, f32[20,28,2048]{2,1,0:T(8,128)} %get-tuple-element.198, s32[]{:T(128)S(6)} %select_n.177), kind=kLoop, calls=%fused_computation.1.clone.1 | loop fusion | flops 819200 | bytes 9830404 | tf_op jit(solution)/shard_map/while/body/eval_jaxpr/add | solution.py:93
  217.0 14.2 %dynamic_update_slice.12 = f32[20,28,2048]{2,1,0:T(8,128)} dynamic-update-slice(f32[20,28,2048]{2,1,0:T(8,128)} %get-tuple-element.198, f32[20,20,2048]{2,1,0:T(8,128)} %dynamic-slice_add_fusion.2, s32[]{:T(128)} %constant.262.clone.1..sunk, s32[]{:T(128)S(6)} %select_n.177, s32[]{:T(128)} %constant.262.clone.1..sunk) | dynamic-update-slice | bytes 6553604 | tf_op jit(solution)/shard_map/while/body/eval_jaxpr/dynamic_update_slice | solution.py:93
  231.2 5.1 %copy.215 = bf16[20,28,2048]{2,0,1:T(8,128)(2,1)S(1)} copy(f32[20,28,2048]{2,1,0:T(8,128)} %get-tuple-element.139) | data formatting | bytes 6881280 | tf_op jit(solution)/shard_map/while | solution.py:95
  242.0 4.2 %slice.170 = f32[20,16,2048]{2,1,0:T(8,128)} slice(f32[20,28,2048]{2,1,0:T(8,128)} %get-tuple-element.139), slice={[0:20], [6:22], [0:2048]} | slice | bytes 5242880 | tf_op jit(solution)/shard_map/slice | solution.py:237
  247.7 4.4 %collective-permute-start.5 = (bf16[20,6,2048]{2,0,1:T(8,128)(2,1)}, bf16[20,6,2048]{2,0,1:T(8,128)(2,1)}, u32[]{:S(2)}, u32[]{:S(2)}) collective-permute-start(bf16[20,6,2048]{2,0,1:T(8,128)(2,1)} %get-tuple-element.148), channel_id=1, source_target_pairs={{0,1},{1,2},{2,3},{3,4},{4,5},{5,6},{6,7},{8,9},{9,10},{10,11},{11... | collective-permute-start | bytes 1474568 | tf_op jit(solution)/shard_map/ppermute | solution.py:29
  254.0 6.2 %scatter-add.14 = f32[20,16,2048]{2,1,0:T(8,128)} dynamic-update-slice(f32[20,16,2048]{2,1,0:T(8,128)} %slice.170, f32[20,6,2048]{2,1,0:T(8,128)S(1)} %convert_add_fusion, s32[]{:T(128)} %constant.262.clone.1, s32[]{:T(128)} %constant.280.clone.1, s32[]{:T(128)} %constant.262.clone.1) | dynamic-update-slice | bytes 1966084 | tf_op jit(solution)/shard_map/scatter-add | solution.py:240
  262.0 7.0 %scatter-add.15 = f32[20,16,2048]{2,1,0:T(8,128)} dynamic-update-slice(f32[20,16,2048]{2,1,0:T(8,128)} %scatter-add.14, f32[20,6,2048]{2,1,0:T(8,128)S(1)} %slice_add_fusion, s32[]{:T(128)} %constant.262.clone.1, s32[]{:T(128)} %constant.262.clone.1, s32[]{:T(128)} %constant.262.clone.1) | dynamic-update-slice | bytes 1966084 | tf_op jit(solution)/shard_map/scatter-add | solution.py:240
  271.1 3.4 %collective-permute-start.6 = (bf16[6,16,2048]{2,1,0:T(8,128)(2,1)S(1)}, bf16[6,16,2048]{2,1,0:T(8,128)(2,1)S(1)}, u32[]{:S(2)}, u32[]{:S(2)}) collective-permute-start(bf16[6,16,2048]{2,1,0:T(8,128)(2,1)S(1)} %get-tuple-element.153), channel_id=1, source_target_pairs={{8,0},{16,8},{24,16},{9,1},{17,9},{25,17},{10,2},{18,10},{26,18},{... | collective-permute-start | bytes 1179656 | tf_op jit(solution)/shard_map/ppermute | solution.py:29
  275.7 20.7 %all-reduce.6.cloned.1.call-done = f32[32,2048]{1,0:T(8,128)} async-done(((f32[32,2048]{1,0:T(8,128)}), f32[32,2048]{1,0:T(8,128)}) %all-reduce.6.cloned.1.call-update) | async-done | bytes 262160 | tf_op jit(solution)/shard_map/psum | solution.py:247
  302.4 9.4 %collective-permute-done.7 = bf16[6,16,2048]{2,1,0:T(8,128)(2,1)S(1)} collective-permute-done((bf16[6,16,2048]{2,1,0:T(8,128)(2,1)S(1)}, bf16[6,16,2048]{2,1,0:T(8,128)(2,1)S(1)}, u32[]{:S(2)}, u32[]{:S(2)}) %collective-permute-start.7) | collective-permute-done | bytes 393248 | tf_op jit(solution)/shard_map/ppermute | solution.py:29
  (141 shorter events, 70.0 us)
Async XLA Ops:
  7.2 75.0 %copy-start = (bf16[1024,1024]{1,0:T(8,128)(2,1)S(1)}, bf16[1024,1024]{1,0:T(8,128)(2,1)}, u32[]{:S(2)}) copy-start(bf16[1024,1024]{1,0:T(8,128)(2,1)} %param.18) | copy-start | bytes 6291460
  7.2 244.9 %all-reduce.4.cloned.1.call-start = ((), (), s32[]{:S(2)}) async-start(), calls=%async_computation | async-start | bytes 524288 | tf_op jit(solution)/shard_map/psum | solution.py:247
  9.5 12.3 %copy-start.20 = (s32[32]{0:T(128)S(1)}, s32[32]{0:T(128)}, u32[]{:S(2)}) copy-start(s32[32]{0:T(128)} %param.22) | copy-start | bytes 388
  11.6 64.4 %copy-start.18 = (bf16[8,16,1024]{2,1,0:T(8,128)(2,1)S(1)}, bf16[8,16,1024]{2,1,0:T(8,128)(2,1)}, u32[]{:S(2)}) copy-start(bf16[8,16,1024]{2,1,0:T(8,128)(2,1)} %param.23) | copy-start | bytes 786436
  12.8 69.8 %collective-permute-start = (bf16[6,16,2048]{2,0,1:T(8,128)(2,1)}, bf16[6,16,2048]{2,0,1:T(8,128)(2,1)}, u32[]{:S(2)}, u32[]{:S(2)}) collective-permute-start(bf16[6,16,2048]{2,0,1:T(8,128)(2,1)} %copy.132), channel_id=1, source_target_pairs={{0,8},{8,16},{16,24},{1,9},{9,17},{17,25},{2,10},{10,18},{18,26},{... | collective-permute-start | bytes 1179656 | tf_op jit(solution)/shard_map/ppermute | solution.py:18
  17.2 65.4 %collective-permute-start.1 = (bf16[6,16,2048]{2,0,1:T(8,128)(2,1)}, bf16[6,16,2048]{2,0,1:T(8,128)(2,1)}, u32[]{:S(2)}, u32[]{:S(2)}) collective-permute-start(bf16[6,16,2048]{2,0,1:T(8,128)(2,1)} %copy.133), channel_id=1, source_target_pairs={{8,0},{16,8},{24,16},{9,1},{17,9},{25,17},{10,2},{18,10},{26,18},{... | collective-permute-start | bytes 1179656 | tf_op jit(solution)/shard_map/ppermute | solution.py:21
  76.0 6.1 %copy-start.9 = (bf16[8,16,1024]{2,1,0:T(8,128)(2,1)S(1)}, bf16[8,16,1024]{2,1,0:T(8,128)(2,1)}, u32[]{:S(2)}) copy-start(bf16[8,16,1024]{2,1,0:T(8,128)(2,1)} %param.17) | copy-start | bytes 786436
  82.1 0.8 copy-start.6
  85.7 15.3 %collective-permute-start.2 = (bf16[20,6,2048]{2,0,1:T(8,128)(2,1)}, bf16[20,6,2048]{2,0,1:T(8,128)(2,1)}, u32[]{:S(2)}, u32[]{:S(2)}) collective-permute-start(bf16[20,6,2048]{2,0,1:T(8,128)(2,1)} %get-tuple-element.150), channel_id=1, source_target_pairs={{0,1},{1,2},{2,3},{3,4},{4,5},{5,6},{6,7},{8,9},{9,10},{10,11},{11... | collective-permute-start | bytes 1474568 | tf_op jit(solution)/shard_map/ppermute | solution.py:18
  87.8 13.1 %collective-permute-start.3 = (bf16[20,6,2048]{2,0,1:T(8,128)(2,1)}, bf16[20,6,2048]{2,0,1:T(8,128)(2,1)}, u32[]{:S(2)}, u32[]{:S(2)}) collective-permute-start(bf16[20,6,2048]{2,0,1:T(8,128)(2,1)} %get-tuple-element.151), channel_id=1, source_target_pairs={{1,0},{2,1},{3,2},{4,3},{5,4},{6,5},{7,6},{9,8},{10,9},{11,10},{12... | collective-permute-start | bytes 1474568 | tf_op jit(solution)/shard_map/ppermute | solution.py:21
  94.7 4.8 %copy-start.13 = (bf16[32,16,64]{2,1,0:T(8,128)(2,1)S(1)}, bf16[32,16,64]{2,1,0:T(8,128)(2,1)}, u32[]{:S(2)}) copy-start(bf16[32,16,64]{2,1,0:T(8,128)(2,1)} %reshape.508) | copy-start | bytes 196612
  132.8 1.2 copy-start.11
  132.8 1.7 copy-start.19
  134.0 1.0 copy-start.17
  135.0 3.0 copy-start.10
  135.0 3.0 copy-start.15
  146.0 6.6 %copy-start.7 = (bf16[2,64,16,64]{1,3,2,0:T(8,128)(2,1)S(1)}, bf16[2,64,16,64]{1,3,2,0:T(8,128)(2,1)}, u32[]{:S(2)}) copy-start(bf16[2,64,16,64]{1,3,2,0:T(8,128)(2,1)} %copy.159) | copy-start | bytes 786436
  152.6 143.7 %all-reduce.6.cloned.1.call-start = ((), (), s32[]{:S(2)}) async-start(), calls=%async_computation.1 | async-start | bytes 524288 | tf_op jit(solution)/shard_map/psum | solution.py:247
  231.2 7.6 %copy-start.1 = (bf16[2,400,1024]{1,2,0:T(8,128)(2,1)S(1)}, bf16[2,400,1024]{1,2,0:T(8,128)(2,1)}, u32[]{:S(2)}) copy-start(bf16[2,400,1024]{1,2,0:T(8,128)(2,1)} %copy.138) | copy-start | bytes 4915204
  231.2 7.6 %copy-start.5 = (bf16[2,16,64,400]{3,2,1,0:T(8,128)(2,1)S(1)}, bf16[2,16,64,400]{3,2,1,0:T(8,128)(2,1)}, u32[]{:S(2)}) copy-start(bf16[2,16,64,400]{3,2,1,0:T(8,128)(2,1)} %multiply_convert_fusion) | copy-start | bytes 4915204
  231.2 7.6 %copy-start.8 = (f32[2,64,16,64]{1,3,2,0:T(8,128)S(1)}, f32[2,64,16,64]{1,3,2,0:T(8,128)}, u32[]{:S(2)}) copy-start(f32[2,64,16,64]{1,3,2,0:T(8,128)} %convolution_bitcast_fusion) | copy-start | bytes 1572868
  237.5 14.6 %collective-permute-start.4 = (bf16[20,6,2048]{2,0,1:T(8,128)(2,1)}, bf16[20,6,2048]{2,0,1:T(8,128)(2,1)}, u32[]{:S(2)}, u32[]{:S(2)}) collective-permute-start(bf16[20,6,2048]{2,0,1:T(8,128)(2,1)} %get-tuple-element.149), channel_id=1, source_target_pairs={{1,0},{2,1},{3,2},{4,3},{5,4},{6,5},{7,6},{9,8},{10,9},{11,10},{12... | collective-permute-start | bytes 1474568 | tf_op jit(solution)/shard_map/ppermute | solution.py:29
  242.0 4.2 %copy-start.16 = (bf16[2,64,16,64]{1,3,2,0:T(8,128)(2,1)S(1)}, bf16[2,64,16,64]{1,3,2,0:T(8,128)(2,1)}, u32[]{:S(2)}) copy-start(bf16[2,64,16,64]{1,3,2,0:T(8,128)(2,1)} %get-tuple-element.165) | copy-start | bytes 786436
  247.7 12.5 %collective-permute-start.5 = (bf16[20,6,2048]{2,0,1:T(8,128)(2,1)}, bf16[20,6,2048]{2,0,1:T(8,128)(2,1)}, u32[]{:S(2)}, u32[]{:S(2)}) collective-permute-start(bf16[20,6,2048]{2,0,1:T(8,128)(2,1)} %get-tuple-element.148), channel_id=1, source_target_pairs={{0,1},{1,2},{2,3},{3,4},{4,5},{5,6},{6,7},{8,9},{9,10},{10,11},{11... | collective-permute-start | bytes 1474568 | tf_op jit(solution)/shard_map/ppermute | solution.py:29
  269.0 5.5 %copy-start.2 = (bf16[1024,1024]{1,0:T(8,128)(2,1)S(1)}, bf16[1024,1024]{1,0:T(8,128)(2,1)}, u32[]{:S(2)}) copy-start(bf16[1024,1024]{1,0:T(8,128)(2,1)} %param.21) | copy-start | bytes 6291460
  269.0 5.5 %copy-start.14 = (bf16[1,8,2,8,1024]{4,3,2,1,0:T(8,128)(2,1)S(1)}, bf16[1,8,2,8,1024]{4,3,2,1,0:T(8,128)(2,1)}, u32[]{:S(2)}) copy-start(bf16[1,8,2,8,1024]{4,3,2,1,0:T(8,128)(2,1)} %copy.149) | copy-start | bytes 786436
  271.1 30.1 %collective-permute-start.6 = (bf16[6,16,2048]{2,1,0:T(8,128)(2,1)S(1)}, bf16[6,16,2048]{2,1,0:T(8,128)(2,1)S(1)}, u32[]{:S(2)}, u32[]{:S(2)}) collective-permute-start(bf16[6,16,2048]{2,1,0:T(8,128)(2,1)S(1)} %get-tuple-element.153), channel_id=1, source_target_pairs={{8,0},{16,8},{24,16},{9,1},{17,9},{25,17},{10,2},{18,10},{26,18},{... | collective-permute-start | bytes 1179656 | tf_op jit(solution)/shard_map/ppermute | solution.py:29
  298.5 13.7 %copy-start.4 = (bf16[1024,1024]{1,0:T(8,128)(2,1)S(1)}, bf16[1024,1024]{1,0:T(8,128)(2,1)}, u32[]{:S(2)}) copy-start(bf16[1024,1024]{1,0:T(8,128)(2,1)} %param.19) | copy-start | bytes 6291460
  298.5 13.7 %copy-start.12 = (f32[128,1024]{1,0:T(8,128)S(1)}, f32[128,1024]{1,0:T(8,128)}, u32[]{:S(2)}) copy-start(f32[128,1024]{1,0:T(8,128)} %fusion.58) | copy-start | bytes 1572868
  298.5 13.3 %collective-permute-start.7 = (bf16[6,16,2048]{2,1,0:T(8,128)(2,1)S(1)}, bf16[6,16,2048]{2,1,0:T(8,128)(2,1)S(1)}, u32[]{:S(2)}, u32[]{:S(2)}) collective-permute-start(bf16[6,16,2048]{2,1,0:T(8,128)(2,1)S(1)} %get-tuple-element.152), channel_id=1, source_target_pairs={{0,8},{8,16},{16,24},{1,9},{9,17},{17,25},{2,10},{10,18},{18,26},{... | collective-permute-start | bytes 1179656 | tf_op jit(solution)/shard_map/ppermute | solution.py:29
  302.4 10.6 %copy-start.3 = (bf16[1024,1024]{1,0:T(8,128)(2,1)S(1)}, bf16[1024,1024]{1,0:T(8,128)(2,1)}, u32[]{:S(2)}) copy-start(bf16[1024,1024]{1,0:T(8,128)(2,1)} %param.20) | copy-start | bytes 6291460
Sparse Core Ops, SparseCore 0:
  152.7 56.5 all-reduce.3
  252.3 44.0 all-reduce.5
